TPU v7x, 32 devices: a whole 2x2x4 slice. The times are simulated.
32 devices in a mesh: shard: 8 (over z, x), tensor: 4 (over y, core).
Axes of the slice: x: 2, y: 2, z: 4, core: 2. Of those that a mesh axis runs over, the one named last changes fastest.
Arguments:
- wide_weight: bfloat16 [4, 4096, 4096], P(None, 'shard', 'tensor'), may hold values from -6 to 6
- wide_grad: bfloat16 [4, 4096, 4096], P(None, 'shard', 'tensor'), may hold values from -6 to 6
- wide_first: float32 [4, 4096, 256], P(None, ('shard', 'tensor')), may hold values from -4 to 4
- wide_second: float32 [4, 4096, 256], P(None, ('shard', 'tensor')), may hold values from 0.001 to 0.1
- wide_basis: bfloat16 [4, 4096, 256], P(None, 'tensor'), may hold values from -0.09375 to 0.09375
- narrow_weight: bfloat16 [4, 1024, 4096], P(None, 'shard', 'tensor'), may hold values from -6 to 6
- narrow_grad: bfloat16 [4, 1024, 4096], P(None, 'shard', 'tensor'), may hold values from -6 to 6
- narrow_first: float32 [4, 1024, 256], P(None, ('shard', 'tensor')), may hold values from -4 to 4
- narrow_second: float32 [4, 1024, 256], P(None, ('shard', 'tensor')), may hold values from 0.001 to 0.1
- narrow_basis: bfloat16 [4, 4096, 256], P(None, 'tensor'), may hold values from -0.09375 to 0.09375
- vocab_weight: bfloat16 [2, 32000, 4096], P(None, 'shard', 'tensor'), may hold values from -6 to 6
- vocab_grad: bfloat16 [2, 32000, 4096], P(None, 'shard', 'tensor'), may hold values from -6 to 6
- vocab_first: float32 [2, 32000, 256], P(None, ('shard', 'tensor')), may hold values from -4 to 4
- vocab_second: float32 [2, 32000, 256], P(None, ('shard', 'tensor')), may hold values from 0.001 to 0.1
- vocab_basis: bfloat16 [2, 4096, 256], P(None, 'tensor'), may hold values from -0.09375 to 0.09375
Outputs:
- wide_weight_new: bfloat16 [4, 4096, 4096], P(None, 'shard', 'tensor')
- wide_first_new: float32 [4, 4096, 256], P(None, ('shard', 'tensor'))
- wide_second_new: float32 [4, 4096, 256], P(None, ('shard', 'tensor'))
- narrow_weight_new: bfloat16 [4, 1024, 4096], P(None, 'shard', 'tensor')
- narrow_first_new: float32 [4, 1024, 256], P(None, ('shard', 'tensor'))
- narrow_second_new: float32 [4, 1024, 256], P(None, ('shard', 'tensor'))
- vocab_weight_new: bfloat16 [2, 32000, 4096], P(None, 'shard', 'tensor')
- vocab_first_new: float32 [2, 32000, 256], P(None, ('shard', 'tensor'))
- vocab_second_new: float32 [2, 32000, 256], P(None, ('shard', 'tensor'))
All inputs are finite; a program needn't handle non-finite values.
Results may differ from a plain program's by a relative error of at most 0.01.
Values may be sent and summed in bfloat16 or wider, within the bound.
No kernel may reach another device: no remote copies, remote signals or barrier semaphores. Data moves between devices by JAX's collectives and lax.ppermute only.
A program may use at most 192 MiB of HBM per device.

v0:
```python
import functools
import jax
import jax.numpy as jnp
from jax import lax
from jax.sharding import PartitionSpec as P

NS_ITERS = 3
HIGHEST = lax.Precision.HIGHEST


def local_gram(polish):
    return jnp.einsum("sdk,sdl->skl", polish, polish, precision=HIGHEST)


def polish_small(back, gram):
    trace = jnp.einsum("skk->s", gram)
    scale = 1.0 / jnp.sqrt(trace + 1e-06)
    small = gram * (scale * scale)[:, None, None]
    rank = gram.shape[1]
    eye = jnp.eye(rank, dtype=jnp.float32)[None, :, :]
    factor = jnp.broadcast_to(eye, gram.shape)
    for step in range(NS_ITERS):
        square = jnp.einsum("skl,slm->skm", small, small, precision=HIGHEST)
        turn = 3.4445 * eye - 4.775 * small + 2.0315 * square
        factor = jnp.einsum("skl,slm->skm", factor, turn, precision=HIGHEST)
        if step + 1 < NS_ITERS:
            small = jnp.einsum(
                "skl,slm->skm",
                turn,
                jnp.einsum("skl,slm->skm", small, turn, precision=HIGHEST),
                precision=HIGHEST,
            )
    return jnp.einsum("sdk,skl->sdl", back * scale[:, None, None], factor, precision=HIGHEST)


def adam_moments(first, second, projected):
    first_new = 0.9 * first + 0.1 * projected
    second_new = 0.999 * second + 0.001 * projected * projected
    direction = first_new / (1.0 - 0.9**10) / (jnp.sqrt(second_new / (1.0 - 0.999**10)) + 1e-08)
    return (first_new, second_new, direction.astype(jnp.bfloat16))


def split_rows(flat, shapes):
    parts = []
    offset = 0
    for shape in shapes:
        size = 1
        for dim in shape:
            size *= dim
        parts.append(flat[..., offset : offset + size].reshape(flat.shape[:-1] + shape))
        offset += size
    return parts


def per_device(
    tensor_size,
    wide_weight,
    wide_grad,
    wide_first,
    wide_second,
    wide_basis,
    narrow_weight,
    narrow_grad,
    narrow_first,
    narrow_second,
    narrow_basis,
    vocab_weight,
    vocab_grad,
    vocab_first,
    vocab_second,
    vocab_basis,
):
    weights = (wide_weight, narrow_weight, vocab_weight)
    grads = (wide_grad, narrow_grad, vocab_grad)
    firsts = (wide_first, narrow_first, vocab_first)
    seconds = (wide_second, narrow_second, vocab_second)
    olds = (wide_basis, narrow_basis, vocab_basis)
    counts = [grad.shape[0] for grad in grads]
    sketch_terms = [
        jnp.einsum("smc,scr->smr", grad, old, preferred_element_type=jnp.float32).astype(
            jnp.bfloat16
        )
        for grad, old in zip(grads, olds)
    ]
    sketches = lax.psum(tuple(sketch_terms), "tensor")
    back_terms = [
        jnp.einsum("smc,smr->scr", grad, sketch, preferred_element_type=jnp.float32)
        for grad, sketch in zip(grads, sketches)
    ]
    back_all = jnp.concatenate(back_terms, axis=0).astype(jnp.bfloat16)
    backs = lax.psum_scatter(back_all, "shard", scatter_dimension=1, tiled=True).astype(jnp.float32)
    grams = lax.psum(local_gram(backs), ("shard", "tensor"))
    rounded = polish_small(backs, grams).astype(jnp.bfloat16)
    basis_all = lax.all_gather(rounded, "shard", axis=1, tiled=True)
    bases = []
    offset = 0
    for count in counts:
        bases.append(basis_all[offset : offset + count])
        offset += count
    proj_parts = []
    row_shapes = []
    for grad, basis in zip(grads, bases):
        count, rows, cols = grad.shape
        split = grad.reshape(count, tensor_size, rows // tensor_size, cols)
        proj = jnp.einsum("sjmc,scr->jsmr", split, basis, preferred_element_type=jnp.float32)
        row_shapes.append((count, rows // tensor_size, basis.shape[2]))
        proj_parts.append(proj.reshape(tensor_size, -1, basis.shape[2]).astype(jnp.bfloat16))
    proj_all = jnp.concatenate(proj_parts, axis=1)
    proj_mine = lax.psum_scatter(proj_all, "tensor", scatter_dimension=0, tiled=True).reshape(-1)
    projected = [part.astype(jnp.float32) for part in split_rows(proj_mine, row_shapes)]
    results = [
        adam_moments(first, second, proj) for first, second, proj in zip(firsts, seconds, projected)
    ]
    dir_all = jnp.concatenate([result[2].reshape(-1) for result in results])
    dir_gathered = lax.all_gather(dir_all, "tensor", axis=0, tiled=False)
    directions = split_rows(dir_gathered, row_shapes)
    outputs = []
    for weight, direction, basis, result in zip(weights, directions, bases, results):
        count, rows, cols = weight.shape
        update = jnp.einsum("jsmr,scr->sjmc", direction, basis, preferred_element_type=jnp.float32)
        update = update.reshape(count, rows, cols)
        weight_new = (0.99 * weight.astype(jnp.float32) - 2.0 * update).astype(jnp.bfloat16)
        outputs.append((weight_new, result[0], result[1]))
    return (
        outputs[0][0],
        outputs[0][1],
        outputs[0][2],
        outputs[1][0],
        outputs[1][1],
        outputs[1][2],
        outputs[2][0],
        outputs[2][1],
        outputs[2][2],
    )


def solution(mesh):
    in_specs = (
        P(None, "shard", "tensor"),
        P(None, "shard", "tensor"),
        P(None, ("shard", "tensor"), None),
        P(None, ("shard", "tensor"), None),
        P(None, "tensor", None),
        P(None, "shard", "tensor"),
        P(None, "shard", "tensor"),
        P(None, ("shard", "tensor"), None),
        P(None, ("shard", "tensor"), None),
        P(None, "tensor", None),
        P(None, "shard", "tensor"),
        P(None, "shard", "tensor"),
        P(None, ("shard", "tensor"), None),
        P(None, ("shard", "tensor"), None),
        P(None, "tensor", None),
    )
    out_specs = (
        P(None, "shard", "tensor"),
        P(None, ("shard", "tensor"), None),
        P(None, ("shard", "tensor"), None),
        P(None, "shard", "tensor"),
        P(None, ("shard", "tensor"), None),
        P(None, ("shard", "tensor"), None),
        P(None, "shard", "tensor"),
        P(None, ("shard", "tensor"), None),
        P(None, ("shard", "tensor"), None),
    )
    return jax.shard_map(
        functools.partial(per_device, mesh.shape["tensor"]),
        mesh=mesh,
        in_specs=in_specs,
        out_specs=out_specs,
        check_vma=False,
    )
```

profile of v0, /device:TPU:0, one launch (start us, length us, event | category | flops | bytes accessed | tf_op | source)
XLA Modules:
  0.0 731.9 jit_solution(9271300986264332978)
XLA Ops:
  7.2 3.2 convolution_convert_fusion.4
  10.4 4.5 convolution_convert_fusion.2
  14.9 12.1 %convolution_convert_fusion = bf16[2,4000,256]{2,1,0:T(8,128)(2,1)} fusion(bf16[2,4000,1024]{2,1,0:T(8,128)(2,1)} %param.26, bf16[2,1024,256]{2,1,0:T(8,128)(2,1)S(1)} %copy-done.16), kind=kOutput, calls=%fused_computation.5 | convolution fusion | flops 4196352000 | bytes 21528576 | tf_op jit(solution)/shard_map/smc,scr->smr/dot_general | solution.py:80
  27.4 108.1 %all-reduce.6.cloned.1.call-done = (bf16[2,4000,256]{2,1,0:T(8,128)(2,1)}, bf16[4,128,256]{2,1,0:T(8,128)(2,1)}, bf16[4,512,256]{2,1,0:T(8,128)(2,1)}) async-done(((bf16[2,4000,256]{2,1,0:T(8,128)(2,1)}, bf16[4,128,256]{2,1,0:T(8,128)(2,1)}, bf16[4,512,256]{2,1,0:T(8,128)(2,1)}), (bf16[2,4000,256]{2,1,0:T(8,128)(2,1)}, bf16[4,128,256]{2,1,0:T(8,128)(2,1)}, ...) | async-done | bytes 5406736 | tf_op jit(solution)/shard_map/psum | solution.py:85
  135.5 11.6 %fusion.32 = bf16[2,1024,256]{1,2,0:T(8,128)(2,1)S(1)} fusion(bf16[2,4000,256]{2,1,0:T(8,128)(2,1)} %get-tuple-element.9, bf16[2,4000,1024]{2,1,0:T(8,128)(2,1)} %param.26), kind=kOutput, calls=%fused_computation.55 | convolution fusion | flops 4194828288 | bytes 21528576 | tf_op jit(solution)/shard_map/smc,smr->scr/dot_general | solution.py:87
  149.6 2.9 pad_maximum_fusion.1
  152.5 11.6 %copy.51 = bf16[10,1024,256]{2,0,1:T(8,128)(2,1)} copy(bf16[10,1024,256]{1,2,0:T(8,128)(2,1)} %pad_maximum_fusion.1) | data formatting | bytes 10485760
  164.1 9.2 %copy.53 = bf16[128,8,10,256]{3,1,2,0:T(8,128)(2,1)} copy(bf16[128,8,10,256]{3,2,1,0:T(8,128)(2,1)} %bitcast.110) | data formatting | bytes 10485760
  173.4 103.0 %reduce-scatter.7.cloned.1.call-done = bf16[128,2560]{1,0:T(8,128)(2,1)} async-done(((bf16[1024,2560]{1,0:T(8,128)(2,1)}), bf16[128,2560]{1,0:T(8,128)(2,1)}) %reduce-scatter.7.cloned.1.call-update) | async-done | bytes 655376
  281.4 137.8 %all-reduce.4.cloned.1.call-done = f32[10,256,256]{2,1,0:T(8,128)} async-done(((f32[10,256,256]{2,1,0:T(8,128)}), f32[10,256,256]{2,1,0:T(8,128)}) %all-reduce.4.cloned.1.call-update) | async-done | bytes 2621456 | tf_op jit(solution)/shard_map/psum | solution.py:92
  421.8 3.1 fusion.22
  424.9 3.5 fusion.15
  428.3 3.3 fusion.14
  431.7 3.1 fusion.94
  434.8 3.3 fusion.9
  438.0 2.8 fusion.16
  440.8 3.3 fusion.10
  444.1 3.5 fusion.8
  450.2 3.2 fusion.3
  453.5 3.3 convolution_convert_fusion.3
  456.8 84.8 %all-gather.4.cloned.1.call-done = bf16[10,1024,256]{2,1,0:T(8,128)(2,1)} async-done(((bf16[10,128,256]{2,1,0:T(8,128)(2,1)}), bf16[10,1024,256]{2,1,0:T(8,128)(2,1)}) %all-gather.4.cloned.1.call-update) | async-done | bytes 5242896 | tf_op jit(solution)/shard_map/all_gather | solution.py:94
  544.5 2.9 fusion.31
  547.4 8.3 %convert_bitcast_fusion = bf16[4,2,1000,256]{3,2,0,1:T(8,128)(2,1)S(1)} fusion(bf16[2,4,1000,1024]{3,2,1,0:T(8,128)(2,1)} %bitcast.134, bf16[10,1024,256]{2,1,0:T(8,128)(2,1)} %all-gather.4.cloned.1.call-done), kind=kOutput, calls=%fused_computation.10 | convolution fusion | flops 4196352000 | bytes 21528576 | tf_op jit(solution)/shard_map/sjmc,scr->jsmr/dot_general | solution.py:105
  556.1 2.8 pad_maximum_fusion
  559.3 50.4 %reduce-scatter.5.cloned.1.call-done = bf16[1,2640,256]{2,1,0:T(8,128)(2,1)} async-done(((bf16[4,2640,256]{2,1,0:T(8,128)(2,1)}), bf16[1,2640,256]{2,1,0:T(8,128)(2,1)}) %reduce-scatter.5.cloned.1.call-update) | async-done | bytes 1351696 | tf_op jit(solution)/shard_map/reduce_scatter | solution.py:109
  615.2 3.5 divide_convert_fusion
  621.0 41.5 %all-gather.6.cloned.1.call-done = bf16[2703360]{0:T(1024)(128)(2,1)} async-done(((bf16[675840]{0:T(1024)(128)(2,1)}), bf16[2703360]{0:T(1024)(128)(2,1)}) %all-gather.6.cloned.1.call-update) | async-done | bytes 5406736 | tf_op jit(solution)/shard_map/all_gather | solution.py:115
  662.5 6.9 reshape.109
  676.2 4.7 broadcast_multiply_fusion
  680.9 7.2 fusion.1
  688.1 14.3 %convolution_multiply_fusion = f32[2,4,1000,1024]{3,2,1,0:T(8,128)} fusion(bf16[4,2,1000,256]{3,2,1,0:T(8,128)(2,1)S(1)} %bitcast.109, bf16[10,1024,256]{2,1,0:T(8,128)(2,1)} %all-gather.4.cloned.1.call-done), kind=kOutput, calls=%fused_computation.2 | convolution fusion | flops 4202496000 | bytes 37912576 | tf_op jit(solution)/shard_map/jsmr,scr->sjmc/dot_general | solution.py:120
  702.3 22.5 %fusion = bf16[2,4000,1024]{2,1,0:T(8,128)(2,1)} fusion(f32[2,4,1000,1024]{3,2,1,0:T(8,128)} %convolution_multiply_fusion, bf16[2,4000,1024]{2,1,0:T(8,128)(2,1)} %param.25), kind=kLoop, calls=%fused_computation.1 | loop fusion | flops 32768000 | bytes 65536000 | tf_op jit(solution)/shard_map/convert_element_type | solution.py:122
  (87 shorter events, 31.3 us)
Async XLA Ops:
  7.2 3.3 copy-start
  7.2 128.3 %all-reduce.6.cloned.1.call-start = ((), (), s32[]{:S(2)}) async-start(), calls=%async_computation.7 | async-start | bytes 10813440 | tf_op jit(solution)/shard_map/psum | solution.py:85
  10.4 4.5 copy-start.16
  27.0 249.4 %reduce-scatter.7.cloned.1.call-start = ((), (), s32[]{:S(2)}) async-start(), calls=%async_computation.6 | async-start | bytes 5898240
  135.5 11.6 %copy-start.5 = (bf16[4,128,1024]{2,1,0:T(8,128)(2,1)S(1)}, bf16[4,128,1024]{2,1,0:T(8,128)(2,1)}, u32[]{:S(2)}) copy-start(bf16[4,128,1024]{2,1,0:T(8,128)(2,1)} %param.21) | copy-start | bytes 3145732
  135.5 11.6 %copy-start.13 = (bf16[4,128,256]{2,1,0:T(8,128)(2,1)S(1)}, bf16[4,128,256]{2,1,0:T(8,128)(2,1)}, u32[]{:S(2)}) copy-start(bf16[4,128,256]{2,1,0:T(8,128)(2,1)} %get-tuple-element.10) | copy-start | bytes 786436
  135.5 12.4 %copy-start.3 = (bf16[4,512,1024]{2,1,0:T(8,128)(2,1)S(1)}, bf16[4,512,1024]{2,1,0:T(8,128)(2,1)}, u32[]{:S(2)}) copy-start(bf16[4,512,1024]{2,1,0:T(8,128)(2,1)} %param.16) | copy-start | bytes 12582916
  147.0 1.2 copy-start.7
  173.4 245.9 %all-reduce.4.cloned.1.call-start = ((), (), s32[]{:S(2)}) async-start(), calls=%async_computation.2 | async-start | bytes 5242880 | tf_op jit(solution)/shard_map/psum | solution.py:92
  280.8 260.9 %all-gather.4.cloned.1.call-start = ((), (), s32[]{:S(2)}) async-start(), calls=%async_computation.3 | async-start | bytes 5898240 | tf_op jit(solution)/shard_map/all_gather | solution.py:94
  419.3 2.5 copy-start.2
  456.8 152.9 %reduce-scatter.5.cloned.1.call-start = ((), (), s32[]{:S(2)}) async-start(), calls=%async_computation.4 | async-start | bytes 6758400 | tf_op jit(solution)/shard_map/reduce_scatter | solution.py:109
  541.7 2.8 copy-start.4
  558.8 51.7 %copy-start.14 = (f32[4,32,256]{2,1,0:T(8,128)S(1)}, f32[4,32,256]{2,1,0:T(8,128)}, u32[]{:S(2)}) copy-start(f32[4,32,256]{2,1,0:T(8,128)} %param.22) | copy-start | bytes 393220
  558.8 51.7 %copy-start.15 = (f32[4,32,256]{2,1,0:T(8,128)S(1)}, f32[4,32,256]{2,1,0:T(8,128)}, u32[]{:S(2)}) copy-start(f32[4,32,256]{2,1,0:T(8,128)} %param.23) | copy-start | bytes 393220
  558.8 53.5 %copy-start.11 = (f32[4,128,256]{2,1,0:T(8,128)S(1)}, f32[4,128,256]{2,1,0:T(8,128)}, u32[]{:S(2)}) copy-start(f32[4,128,256]{2,1,0:T(8,128)} %param.17) | copy-start | bytes 1572868
  558.8 53.5 %copy-start.12 = (f32[4,128,256]{2,1,0:T(8,128)S(1)}, f32[4,128,256]{2,1,0:T(8,128)}, u32[]{:S(2)}) copy-start(f32[4,128,256]{2,1,0:T(8,128)} %param.18) | copy-start | bytes 1572868
  558.9 103.6 %all-gather.6.cloned.1.call-start = ((), (), s32[]{:S(2)}) async-start(), calls=%async_computation.5 | async-start | bytes 6758400 | tf_op jit(solution)/shard_map/all_gather | solution.py:115
  612.3 1.6 slice-start.5
  612.3 2.3 copy-start.8
  612.3 2.9 copy-start.9
  669.4 0.9 slice-start
  669.4 2.3 slice-start.2
  669.4 4.1 slice-start.3
  671.7 1.7 slice-start.1
  671.7 2.0 slice-start.4
  673.5 1.3 copy-start.10
  676.2 4.7 copy-start.6
  702.3 22.5 %copy-start.1 = (bf16[4,1024,256]{2,1,0:T(8,128)(2,1)S(1)}, bf16[4,1024,256]{2,1,0:T(8,128)(2,1)}, u32[]{:S(2)}) copy-start(bf16[4,1024,256]{2,1,0:T(8,128)(2,1)} %param.19) | copy-start | bytes 6291460
Sparse Core Ops, SparseCore 0:
  27.2 108.2 all-reduce.5
  173.5 102.8 reduce-scatter.6
  283.3 135.8 all-reduce.3
  456.9 84.6 all-gather.3
  559.0 50.6 reduce-scatter.4
  621.1 41.3 all-gather.5
where the time goes:
time: 737 us; the launch traced here: 732 us
  waiting for transfers between devices  526 us (71%)
  matrix products  103 us (14%)
  other arithmetic  45.9 us (6%)
  local copies, waits for them, and re-layouts  40.7 us (6%)
  between operations  14.7 us (2%)
    psum x1, waiting for transfers between devices, per_device(): grams = lax.psum(local_gram(backs), ('shard', 'tensor'))  138 us
    psum x1, waiting for transfers between devices, per_device(): sketches = lax.psum(tuple(sketch_terms), 'tensor')  108 us
    unnamed x7, waiting for transfers between devices  103 us
    all_gather x1, waiting for transfers between devices, per_device(): basis_all = lax.all_gather(rounded, 'shard', axis=1, tiled=True)  84.8 us
    reduce_scatter x1, waiting for transfers between devices, per_device(): lax.psum_scatter(proj_all, 'tensor', scatter_dimension=0, tiled=True)  50.4 us
    all_gather x1, waiting for transfers between devices, per_device(): dir_gathered = lax.all_gather(dir_all, 'tensor', axis=0, tiled=False)  41.5 us
    convert_element_type x3, other arithmetic, per_device(): (0.99 * weight.astype(jnp.float32) - 2.0 * update).astype(jnp.bfloat16)  31.1 us
    unnamed x48, local copies, waits for them, and re-layouts  28.2 us
  transfers between devices with their start and end apart: 6, of which 6 were waited for; matrix products, arithmetic and copies ran while one was open for 0% of the time, Pallas kernels for 0%

commit v1 on v0

--- a/solution.py
+++ b/solution.py
@@ -91,7 +91,14 @@
     backs = lax.psum_scatter(back_all, "shard", scatter_dimension=1, tiled=True).astype(jnp.float32)
     grams = lax.psum(local_gram(backs), ("shard", "tensor"))
     rounded = polish_small(backs, grams).astype(jnp.bfloat16)
-    basis_all = lax.all_gather(rounded, "shard", axis=1, tiled=True)
+    ring = [rounded]
+    for hop in range(7):
+        ring.append(lax.ppermute(ring[-1], "shard", [(dev, (dev + 1) % 8) for dev in range(8)]))
+    basis_all = jnp.roll(
+        jnp.concatenate(ring[::-1], axis=1),
+        (lax.axis_index("shard") + 1) * ring[0].shape[1],
+        axis=1,
+    )
     bases = []
     offset = 0
     for count in counts:

time: 737 us -> 772 us (1.047)
  waiting for transfers between devices: 526 us -> 547 us
  local copies, waits for them, and re-layouts: 40.7 us -> 53.5 us
    ppermute x0 -> x7, waiting for transfers between devices: none -> 106 us  [per_device(): lax.ppermute(ring[-1], 'shard', [(dev, (dev + 1) % 8) for dev in range(8)])]
    all_gather x1 -> x0, waiting for transfers between devices: 84.8 us -> none  [per_device(): basis_all = lax.all_gather(rounded, 'shard', axis=1, tiled=True)]
    unnamed x48 -> x77, local copies, waits for them, and re-layouts: 28.2 us -> 41.3 us
    unnamed x7 -> x6, waiting for transfers between devices: 103 us -> 103 us
  transfers between devices with their start and end apart: 6 -> 12, of which waited for: 6 -> 12; matrix products, arithmetic and copies ran while one was open for 0% -> 0% of each run, Pallas kernels for 0% -> 0%
where the time goes in v1:
time: 772 us; the launch traced here: 766 us
  waiting for transfers between devices  547 us (71%)
  matrix products  102 us (13%)
  local copies, waits for them, and re-layouts  53.5 us (7%)
  other arithmetic  45.9 us (6%)
  between operations  14.6 us (2%)
    psum x1, waiting for transfers between devices, per_device(): grams = lax.psum(local_gram(backs), ('shard', 'tensor'))  138 us
    psum x1, waiting for transfers between devices, per_device(): sketches = lax.psum(tuple(sketch_terms), 'tensor')  108 us
    ppermute x7, waiting for transfers between devices, per_device(): lax.ppermute(ring[-1], 'shard', [(dev, (dev + 1) % 8) for dev in range(8)])  106 us
    unnamed x6, waiting for transfers between devices  103 us
    reduce_scatter x1, waiting for transfers between devices, per_device(): lax.psum_scatter(proj_all, 'tensor', scatter_dimension=0, tiled=True)  50.3 us
    all_gather x1, waiting for transfers between devices, per_device(): dir_gathered = lax.all_gather(dir_all, 'tensor', axis=0, tiled=False)  41.5 us
    unnamed x77, local copies, waits for them, and re-layouts  41.3 us
    convert_element_type x3, other arithmetic, per_device(): (0.99 * weight.astype(jnp.float32) - 2.0 * update).astype(jnp.bfloat16)  31.1 us
  transfers between devices with their start and end apart: 12, of which 12 were waited for; matrix products, arithmetic and copies ran while one was open for 0% of the time, Pallas kernels for 0%

profile of v1, /device:TPU:0, one launch (start us, length us, event | category | flops | bytes accessed | tf_op | source)
XLA Modules:
  0.0 766.3 jit_solution(5557348728912901871)
XLA Ops:
  7.2 3.2 convolution_convert_fusion.4
  10.4 4.5 convolution_convert_fusion.2
  14.9 12.1 %convolution_convert_fusion = bf16[2,4000,256]{2,1,0:T(8,128)(2,1)} fusion(bf16[2,4000,1024]{2,1,0:T(8,128)(2,1)} %param.26, bf16[2,1024,256]{2,1,0:T(8,128)(2,1)S(1)} %copy-done.25), kind=kOutput, calls=%fused_computation.5 | convolution fusion | flops 4196352000 | bytes 21528576 | tf_op jit(solution)/shard_map/smc,scr->smr/dot_general | solution.py:80
  27.4 108.1 %all-reduce.6.cloned.1.call-done = (bf16[2,4000,256]{2,1,0:T(8,128)(2,1)}, bf16[4,128,256]{2,1,0:T(8,128)(2,1)}, bf16[4,512,256]{2,1,0:T(8,128)(2,1)}) async-done(((bf16[2,4000,256]{2,1,0:T(8,128)(2,1)}, bf16[4,128,256]{2,1,0:T(8,128)(2,1)}, bf16[4,512,256]{2,1,0:T(8,128)(2,1)}), (bf16[2,4000,256]{2,1,0:T(8,128)(2,1)}, bf16[4,128,256]{2,1,0:T(8,128)(2,1)}, ...) | async-done | bytes 5406736 | tf_op jit(solution)/shard_map/psum | solution.py:85
  135.5 11.6 %fusion.32 = bf16[2,1024,256]{1,2,0:T(8,128)(2,1)S(1)} fusion(bf16[2,4000,256]{2,1,0:T(8,128)(2,1)} %get-tuple-element.9, bf16[2,4000,1024]{2,1,0:T(8,128)(2,1)} %param.26), kind=kOutput, calls=%fused_computation.55 | convolution fusion | flops 4194828288 | bytes 21528576 | tf_op jit(solution)/shard_map/smc,smr->scr/dot_general | solution.py:87
  152.6 11.6 %copy.51 = bf16[10,1024,256]{2,0,1:T(8,128)(2,1)} copy(bf16[10,1024,256]{1,2,0:T(8,128)(2,1)} %pad_maximum_fusion.1) | data formatting | bytes 10485760
  164.2 9.2 %copy.53 = bf16[128,8,10,256]{3,1,2,0:T(8,128)(2,1)} copy(bf16[128,8,10,256]{3,2,1,0:T(8,128)(2,1)} %bitcast.110) | data formatting | bytes 10485760
  173.5 103.0 %reduce-scatter.7.cloned.1.call-done = bf16[128,2560]{1,0:T(8,128)(2,1)} async-done(((bf16[1024,2560]{1,0:T(8,128)(2,1)}), bf16[128,2560]{1,0:T(8,128)(2,1)}) %reduce-scatter.7.cloned.1.call-update) | async-done | bytes 655376
  281.5 137.8 %all-reduce.4.cloned.1.call-done = f32[10,256,256]{2,1,0:T(8,128)} async-done(((f32[10,256,256]{2,1,0:T(8,128)}), f32[10,256,256]{2,1,0:T(8,128)}) %all-reduce.4.cloned.1.call-update) | async-done | bytes 2621456 | tf_op jit(solution)/shard_map/psum | solution.py:92
  424.9 3.5 fusion.15
  428.4 3.3 fusion.14
  434.8 3.3 fusion.9
  440.9 3.3 fusion.10
  444.2 3.5 fusion.8
  450.3 3.2 fusion.3
  457.4 16.3 %collective-permute-done = bf16[10,128,256]{2,1,0:T(8,128)(2,1)S(1)} collective-permute-done((bf16[10,128,256]{2,1,0:T(8,128)(2,1)S(1)}, bf16[10,128,256]{2,1,0:T(8,128)(2,1)S(1)}, u32[]{:S(2)}, u32[]{:S(2)}) %collective-permute-start) | collective-permute-done | bytes 655392 | tf_op jit(solution)/shard_map/ppermute | solution.py:96
  473.7 16.7 %collective-permute-done.1 = bf16[10,128,256]{2,1,0:T(8,128)(2,1)S(1)} collective-permute-done((bf16[10,128,256]{2,1,0:T(8,128)(2,1)S(1)}, bf16[10,128,256]{2,1,0:T(8,128)(2,1)S(1)}, u32[]{:S(2)}, u32[]{:S(2)}) %collective-permute-start.1) | collective-permute-done | bytes 655392 | tf_op jit(solution)/shard_map/ppermute | solution.py:96
  491.2 15.8 %collective-permute-done.2 = bf16[10,128,256]{2,1,0:T(8,128)(2,1)S(1)} collective-permute-done((bf16[10,128,256]{2,1,0:T(8,128)(2,1)S(1)}, bf16[10,128,256]{2,1,0:T(8,128)(2,1)S(1)}, u32[]{:S(2)}, u32[]{:S(2)}) %collective-permute-start.2) | collective-permute-done | bytes 655392 | tf_op jit(solution)/shard_map/ppermute | solution.py:96
  507.8 14.8 %collective-permute-done.3 = bf16[10,128,256]{2,1,0:T(8,128)(2,1)S(1)} collective-permute-done((bf16[10,128,256]{2,1,0:T(8,128)(2,1)S(1)}, bf16[10,128,256]{2,1,0:T(8,128)(2,1)S(1)}, u32[]{:S(2)}, u32[]{:S(2)}) %collective-permute-start.3) | collective-permute-done | bytes 655392 | tf_op jit(solution)/shard_map/ppermute | solution.py:96
  523.5 14.1 %collective-permute-done.4 = bf16[10,128,256]{2,1,0:T(8,128)(2,1)S(1)} collective-permute-done((bf16[10,128,256]{2,1,0:T(8,128)(2,1)S(1)}, bf16[10,128,256]{2,1,0:T(8,128)(2,1)S(1)}, u32[]{:S(2)}, u32[]{:S(2)}) %collective-permute-start.4) | collective-permute-done | bytes 655392 | tf_op jit(solution)/shard_map/ppermute | solution.py:96
  538.4 14.9 %collective-permute-done.5 = bf16[10,128,256]{2,1,0:T(8,128)(2,1)} collective-permute-done((bf16[10,128,256]{2,1,0:T(8,128)(2,1)S(1)}, bf16[10,128,256]{2,1,0:T(8,128)(2,1)}, u32[]{:S(2)}, u32[]{:S(2)}) %collective-permute-start.5) | collective-permute-done | bytes 655392 | tf_op jit(solution)/shard_map/ppermute | solution.py:96
  553.6 13.5 %collective-permute-done.6 = bf16[10,128,256]{2,1,0:T(8,128)(2,1)} collective-permute-done((bf16[10,128,256]{2,1,0:T(8,128)(2,1)}, bf16[10,128,256]{2,1,0:T(8,128)(2,1)}, u32[]{:S(2)}, u32[]{:S(2)}) %collective-permute-start.6) | collective-permute-done | bytes 655392 | tf_op jit(solution)/shard_map/ppermute | solution.py:96
  572.9 4.5 copy-done.4
  578.8 8.3 %convert_bitcast_fusion = bf16[4,2,1000,256]{3,2,0,1:T(8,128)(2,1)S(1)} fusion(bf16[2,4,1000,1024]{3,2,1,0:T(8,128)(2,1)} %bitcast.132, bf16[10,2048,256]{2,1,0:T(8,128)(2,1)} %copy-done.7, s32[]{:T(128)S(6)} %add.100, s32[]{:T(128)S(6)} %select_n.18), kind=kOutput, calls=%fused_computation.10 | convolution fusion | flops 4196352000 | bytes 21528584 | tf_op jit(solution)/shard_map/sjmc,scr->jsmr/dot_general | solution.py:112
  590.7 50.3 %reduce-scatter.5.cloned.1.call-done = bf16[1,2640,256]{2,1,0:T(8,128)(2,1)} async-done(((bf16[4,2640,256]{2,1,0:T(8,128)(2,1)}), bf16[1,2640,256]{2,1,0:T(8,128)(2,1)}) %reduce-scatter.5.cloned.1.call-update) | async-done | bytes 1351696 | tf_op jit(solution)/shard_map/reduce_scatter | solution.py:116
  646.6 3.5 divide_convert_fusion
  652.4 41.5 %all-gather.3.cloned.1.call-done = bf16[2703360]{0:T(1024)(128)(2,1)} async-done(((bf16[675840]{0:T(1024)(128)(2,1)}), bf16[2703360]{0:T(1024)(128)(2,1)}) %all-gather.3.cloned.1.call-update) | async-done | bytes 5406736 | tf_op jit(solution)/shard_map/all_gather | solution.py:122
  693.9 7.0 reshape.109
  706.9 6.1 broadcast_multiply_fusion
  713.0 14.3 %convolution_multiply_fusion = f32[2,4,1000,1024]{3,2,1,0:T(8,128)} fusion(bf16[4,2,1000,256]{3,2,1,0:T(8,128)(2,1)S(1)} %bitcast.109, bf16[10,2048,256]{2,1,0:T(8,128)(2,1)} %copy-done.7, s32[]{:T(128)S(6)} %add.100, s32[]{:T(128)S(6)} %select_n.18), kind=kOutput, calls=%fused_computation.2 | convolution fusion | flops 4202496000 | bytes 37912584 | tf_op jit(solution)/shard_map/jsmr,scr->sjmc/dot_general | solution.py:127
  729.9 7.2 fusion.1
  737.1 22.5 %fusion = bf16[2,4000,1024]{2,1,0:T(8,128)(2,1)} fusion(f32[2,4,1000,1024]{3,2,1,0:T(8,128)} %convolution_multiply_fusion, bf16[2,4000,1024]{2,1,0:T(8,128)(2,1)} %param.25), kind=kLoop, calls=%fused_computation.1 | loop fusion | flops 32768000 | bytes 65536000 | tf_op jit(solution)/shard_map/convert_element_type | solution.py:129
  (127 shorter events, 59.3 us)
Async XLA Ops:
  7.2 3.3 copy-start
  7.2 128.3 %all-reduce.6.cloned.1.call-start = ((), (), s32[]{:S(2)}) async-start(), calls=%async_computation.6 | async-start | bytes 10813440 | tf_op jit(solution)/shard_map/psum | solution.py:85
  10.4 4.5 copy-start.25
  27.0 249.4 %reduce-scatter.7.cloned.1.call-start = ((), (), s32[]{:S(2)}) async-start(), calls=%async_computation.5 | async-start | bytes 5898240
  135.5 11.6 %copy-start.5 = (bf16[4,128,1024]{2,1,0:T(8,128)(2,1)S(1)}, bf16[4,128,1024]{2,1,0:T(8,128)(2,1)}, u32[]{:S(2)}) copy-start(bf16[4,128,1024]{2,1,0:T(8,128)(2,1)} %param.21) | copy-start | bytes 3145732
  135.5 11.6 %copy-start.22 = (bf16[4,128,256]{2,1,0:T(8,128)(2,1)S(1)}, bf16[4,128,256]{2,1,0:T(8,128)(2,1)}, u32[]{:S(2)}) copy-start(bf16[4,128,256]{2,1,0:T(8,128)(2,1)} %get-tuple-element.10) | copy-start | bytes 786436
  135.5 12.4 %copy-start.3 = (bf16[4,512,1024]{2,1,0:T(8,128)(2,1)S(1)}, bf16[4,512,1024]{2,1,0:T(8,128)(2,1)}, u32[]{:S(2)}) copy-start(bf16[4,512,1024]{2,1,0:T(8,128)(2,1)} %param.16) | copy-start | bytes 12582916
  173.5 245.9 %all-reduce.4.cloned.1.call-start = ((), (), s32[]{:S(2)}) async-start(), calls=%async_computation.2 | async-start | bytes 5242880 | tf_op jit(solution)/shard_map/psum | solution.py:92
  280.8 360.2 %reduce-scatter.5.cloned.1.call-start = ((), (), s32[]{:S(2)}) async-start(), calls=%async_computation.3 | async-start | bytes 6758400 | tf_op jit(solution)/shard_map/reduce_scatter | solution.py:116
  419.4 2.5 copy-start.2
  456.0 17.7 %collective-permute-start = (bf16[10,128,256]{2,1,0:T(8,128)(2,1)S(1)}, bf16[10,128,256]{2,1,0:T(8,128)(2,1)S(1)}, u32[]{:S(2)}, u32[]{:S(2)}) collective-permute-start(bf16[10,128,256]{2,1,0:T(8,128)(2,1)S(1)} %convolution_convert_fusion.3), channel_id=1, source_target_pairs={{0,4},{4,8},{8,12},{12,16},{16,20},{20,24},{24,28},{28,0},{1,5},{5... | collective-permute-start | bytes 1966088 | tf_op jit(solution)/shard_map/ppermute | solution.py:96
  473.7 16.7 %collective-permute-start.1 = (bf16[10,128,256]{2,1,0:T(8,128)(2,1)S(1)}, bf16[10,128,256]{2,1,0:T(8,128)(2,1)S(1)}, u32[]{:S(2)}, u32[]{:S(2)}) collective-permute-start(bf16[10,128,256]{2,1,0:T(8,128)(2,1)S(1)} %collective-permute-done), channel_id=1, source_target_pairs={{0,4},{4,8},{8,12},{12,16},{16,20},{20,24},{24,28},{28,0},{1,5},{5... | collective-permute-start | bytes 1966088 | tf_op jit(solution)/shard_map/ppermute | solution.py:96
  491.2 15.8 %collective-permute-start.2 = (bf16[10,128,256]{2,1,0:T(8,128)(2,1)S(1)}, bf16[10,128,256]{2,1,0:T(8,128)(2,1)S(1)}, u32[]{:S(2)}, u32[]{:S(2)}) collective-permute-start(bf16[10,128,256]{2,1,0:T(8,128)(2,1)S(1)} %collective-permute-done.1), channel_id=1, source_target_pairs={{0,4},{4,8},{8,12},{12,16},{16,20},{20,24},{24,28},{28,0},{1,5},{5... | collective-permute-start | bytes 1966088 | tf_op jit(solution)/shard_map/ppermute | solution.py:96
  507.8 14.8 %collective-permute-start.3 = (bf16[10,128,256]{2,1,0:T(8,128)(2,1)S(1)}, bf16[10,128,256]{2,1,0:T(8,128)(2,1)S(1)}, u32[]{:S(2)}, u32[]{:S(2)}) collective-permute-start(bf16[10,128,256]{2,1,0:T(8,128)(2,1)S(1)} %collective-permute-done.2), channel_id=1, source_target_pairs={{0,4},{4,8},{8,12},{12,16},{16,20},{20,24},{24,28},{28,0},{1,5},{5... | collective-permute-start | bytes 1966088 | tf_op jit(solution)/shard_map/ppermute | solution.py:96
  523.5 14.1 %collective-permute-start.4 = (bf16[10,128,256]{2,1,0:T(8,128)(2,1)S(1)}, bf16[10,128,256]{2,1,0:T(8,128)(2,1)S(1)}, u32[]{:S(2)}, u32[]{:S(2)}) collective-permute-start(bf16[10,128,256]{2,1,0:T(8,128)(2,1)S(1)} %collective-permute-done.3), channel_id=1, source_target_pairs={{0,4},{4,8},{8,12},{12,16},{16,20},{20,24},{24,28},{28,0},{1,5},{5... | collective-permute-start | bytes 1966088 | tf_op jit(solution)/shard_map/ppermute | solution.py:96
  538.4 14.9 %collective-permute-start.5 = (bf16[10,128,256]{2,1,0:T(8,128)(2,1)S(1)}, bf16[10,128,256]{2,1,0:T(8,128)(2,1)}, u32[]{:S(2)}, u32[]{:S(2)}) collective-permute-start(bf16[10,128,256]{2,1,0:T(8,128)(2,1)S(1)} %collective-permute-done.4), channel_id=1, source_target_pairs={{0,4},{4,8},{8,12},{12,16},{16,20},{20,24},{24,28},{28,0},{1,5},{5... | collective-permute-start | bytes 1966088 | tf_op jit(solution)/shard_map/ppermute | solution.py:96
  553.3 13.8 %collective-permute-start.6 = (bf16[10,128,256]{2,1,0:T(8,128)(2,1)}, bf16[10,128,256]{2,1,0:T(8,128)(2,1)}, u32[]{:S(2)}, u32[]{:S(2)}) collective-permute-start(bf16[10,128,256]{2,1,0:T(8,128)(2,1)} %collective-permute-done.5), channel_id=1, source_target_pairs={{0,4},{4,8},{8,12},{12,16},{16,20},{20,24},{24,28},{28,0},{1,5},{5... | collective-permute-start | bytes 1966088 | tf_op jit(solution)/shard_map/ppermute | solution.py:96
  553.5 15.9 %copy-start.15 = (bf16[10,128,256]{2,1,0:T(8,128)(2,1)S(1)}, bf16[10,128,256]{2,1,0:T(8,128)(2,1)}, u32[]{:S(2)}) copy-start(bf16[10,128,256]{2,1,0:T(8,128)(2,1)} %copy-done.14) | copy-start | bytes 1966084
  553.5 16.0 %copy-start.13 = (bf16[10,128,256]{2,1,0:T(8,128)(2,1)S(1)}, bf16[10,128,256]{2,1,0:T(8,128)(2,1)}, u32[]{:S(2)}) copy-start(bf16[10,128,256]{2,1,0:T(8,128)(2,1)} %copy-done.12) | copy-start | bytes 1966084
  553.6 16.0 %copy-start.11 = (bf16[10,128,256]{2,1,0:T(8,128)(2,1)S(1)}, bf16[10,128,256]{2,1,0:T(8,128)(2,1)}, u32[]{:S(2)}) copy-start(bf16[10,128,256]{2,1,0:T(8,128)(2,1)} %copy-done.10) | copy-start | bytes 1966084
  572.3 5.1 copy-start.4
  572.4 6.3 copy-start.7
  590.2 51.7 %copy-start.23 = (f32[4,32,256]{2,1,0:T(8,128)S(1)}, f32[4,32,256]{2,1,0:T(8,128)}, u32[]{:S(2)}) copy-start(f32[4,32,256]{2,1,0:T(8,128)} %param.22) | copy-start | bytes 393220
  590.2 51.7 %copy-start.24 = (f32[4,32,256]{2,1,0:T(8,128)S(1)}, f32[4,32,256]{2,1,0:T(8,128)}, u32[]{:S(2)}) copy-start(f32[4,32,256]{2,1,0:T(8,128)} %param.23) | copy-start | bytes 393220
  590.2 53.6 %copy-start.20 = (f32[4,128,256]{2,1,0:T(8,128)S(1)}, f32[4,128,256]{2,1,0:T(8,128)}, u32[]{:S(2)}) copy-start(f32[4,128,256]{2,1,0:T(8,128)} %param.17) | copy-start | bytes 1572868
  590.2 53.6 %copy-start.21 = (f32[4,128,256]{2,1,0:T(8,128)S(1)}, f32[4,128,256]{2,1,0:T(8,128)}, u32[]{:S(2)}) copy-start(f32[4,128,256]{2,1,0:T(8,128)} %param.18) | copy-start | bytes 1572868
  590.2 103.7 %all-gather.3.cloned.1.call-start = ((), (), s32[]{:S(2)}) async-start(), calls=%async_computation.4 | async-start | bytes 6758400 | tf_op jit(solution)/shard_map/all_gather | solution.py:122
  643.7 2.3 copy-start.17
  643.7 2.9 copy-start.18
  713.0 14.3 %copy-start.19 = (bf16[4,128,1024]{2,1,0:T(8,128)(2,1)S(1)}, bf16[4,128,1024]{2,1,0:T(8,128)(2,1)}, u32[]{:S(2)}) copy-start(bf16[4,128,1024]{2,1,0:T(8,128)(2,1)} %param.20) | copy-start | bytes 3145732
  727.3 2.6 copy-start.6
  737.1 22.5 %copy-start.1 = (bf16[4,1024,256]{2,1,0:T(8,128)(2,1)S(1)}, bf16[4,1024,256]{2,1,0:T(8,128)(2,1)}, u32[]{:S(2)}) copy-start(bf16[4,1024,256]{2,1,0:T(8,128)(2,1)} %param.19) | copy-start | bytes 6291460
  (10 other events, 12.0 us)
Sparse Core Ops, SparseCore 0:
  27.2 108.2 all-reduce.5
  173.6 102.8 reduce-scatter.6
  283.4 135.8 all-reduce.3
  590.3 50.6 reduce-scatter.4
  652.5 41.3 all-gather.2
